TPU v7x, 256 devices: a whole 4x4x8 slice. The times are simulated.
256 devices in a mesh: shard: 64 (over y, z_hi, x), rep: 4 (over z_lo, core).
Axes of the slice: x: 4, y: 4, z: 8 (z_hi: 4, z_lo: 2; z = z_hi * 2 + z_lo), core: 2. Of those that a mesh axis runs over, the one named last changes fastest.
Arguments:
- rows_in: bfloat16 [131072, 2048], P(('shard', 'rep')), may hold values from -24 to 24
- cotangent: bfloat16 [131072, 2048], P(('shard', 'rep')), may hold values from -24 to 24
- expert_counts: int32 [256, 2], P(('shard', 'rep')), may hold values from 0 to 512, as said below
- weights: bfloat16 [2048, 2, 1152], P('shard'), may hold values from -0.125 to 0.125
Outputs:
- rows_out: bfloat16 [131072, 2048], P(('shard', 'rep'))
- rows_grad: bfloat16 [131072, 2048], P(('shard', 'rep'))
- weight_grad: float32 [2048, 2, 1152], P('shard')
Inputs may be any that keep to these rules, and one draw needn't show every extreme that they name: `expert_counts`: on each device the experts' regions, each padded to a multiple of 128 rows, follow one another from row 0 and together fill at most 512 rows; some device fills all 512; one expert on some device holds all 512 rows.
All inputs are finite; a program needn't handle non-finite values.
Results may differ from a plain program's by a relative error of at most 0.0095.
Values may be sent and summed in bfloat16 or wider, within the bound.
No kernel may reach another device: no remote copies, remote signals or barrier semaphores. Data moves between devices by JAX's collectives and lax.ppermute only.
A program may use at most 128 MiB of HBM per device.

v0:
```python
import jax
import jax.numpy as jnp
from jax import lax
from jax.sharding import PartitionSpec as P

BLOCK = 128


def expert_block(inputs, upstream, expert_slab):
    hidden_width = expert_slab.shape[1] // 3
    gate_up = expert_slab[:, : 2 * hidden_width]
    down_t = expert_slab[:, 2 * hidden_width :]
    project = jnp.dot(inputs, gate_up, preferred_element_type=jnp.float32)
    gate_pre = project[:, :hidden_width]
    up_pre = project[:, hidden_width:]
    gate_sigmoid = jax.nn.sigmoid(gate_pre)
    active = gate_pre * gate_sigmoid
    hidden = (active * up_pre).astype(jnp.bfloat16)
    output = lax.dot_general(
        hidden, down_t, (((1,), (1,)), ((), ())), preferred_element_type=jnp.float32
    ).astype(jnp.bfloat16)
    hidden_grad = jnp.dot(upstream, down_t, preferred_element_type=jnp.float32)
    down_grad = lax.dot_general(
        upstream, hidden, (((0,), (0,)), ((), ())), preferred_element_type=jnp.float32
    )
    gate_grad = hidden_grad * up_pre * gate_sigmoid * (1.0 + gate_pre * (1.0 - gate_sigmoid))
    up_grad = hidden_grad * active
    joint_grad = jnp.concatenate([gate_grad, up_grad], axis=1).astype(jnp.bfloat16)
    proj_grad = lax.dot_general(
        inputs, joint_grad, (((0,), (0,)), ((), ())), preferred_element_type=jnp.float32
    )
    input_grad = lax.dot_general(
        joint_grad, gate_up, (((1,), (1,)), ((), ())), preferred_element_type=jnp.float32
    ).astype(jnp.bfloat16)
    return (output, input_grad, jnp.concatenate([proj_grad, down_grad], axis=1))


def alive_rows(counts, total_rows):
    padded = (counts + BLOCK - 1) // BLOCK * BLOCK
    starts = jnp.cumsum(padded) - padded
    position = jnp.arange(total_rows, dtype=jnp.int32)
    inside = (position[:, None] >= starts[None, :]) & (
        position[:, None] < (starts + counts)[None, :]
    )
    return (jnp.any(inside, axis=1), padded, starts)


def run_expert(expert_slab, inputs, upstream, start_row, nblocks, outputs, input_grads):

    def block_step(block_index, state):
        outputs, input_grads, grad_total = state
        row_begin = start_row + block_index * BLOCK
        block_in = lax.dynamic_slice_in_dim(inputs, row_begin, BLOCK, 0)
        block_up = lax.dynamic_slice_in_dim(upstream, row_begin, BLOCK, 0)
        output, input_grad, grad_piece = expert_block(block_in, block_up, expert_slab)
        outputs = lax.dynamic_update_slice_in_dim(outputs, output, row_begin, 0)
        input_grads = lax.dynamic_update_slice_in_dim(input_grads, input_grad, row_begin, 0)
        return (outputs, input_grads, grad_total + grad_piece)

    start_grad = jnp.zeros(expert_slab.shape, jnp.float32)
    return lax.fori_loop(jnp.int32(0), nblocks, block_step, (outputs, input_grads, start_grad))


def reduce_grads(grads):
    partial_sum = lax.psum_scatter(grads, "shard", scatter_dimension=0, tiled=True)
    return lax.psum(partial_sum.astype(jnp.bfloat16), "rep").astype(jnp.float32)


def local(rows_in, cotangent, expert_counts, weights):
    counts = expert_counts[0]
    alive, padded, starts = alive_rows(counts, rows_in.shape[0])
    inputs = jnp.where(alive[:, None], rows_in, jnp.zeros_like(rows_in))
    upstream = jnp.where(alive[:, None], cotangent, jnp.zeros_like(cotangent))
    outputs = jnp.zeros_like(rows_in)
    input_grads = jnp.zeros_like(rows_in)
    experts = weights.shape[1]
    pieces = []
    gathered = lax.all_gather(weights, "shard", axis=0, tiled=True)
    for expert in range(experts):
        outputs, input_grads, grad_total = run_expert(
            gathered[:, expert],
            inputs,
            upstream,
            starts[expert],
            padded[expert] // BLOCK,
            outputs,
            input_grads,
        )
        pieces.append(grad_total)
    reduced = reduce_grads(jnp.stack(pieces, axis=1))
    return (outputs, input_grads, reduced)


def solution(mesh):
    in_specs = (
        P(("shard", "rep"), None),
        P(("shard", "rep"), None),
        P(("shard", "rep"), None),
        P("shard", None, None),
    )
    out_specs = (P(("shard", "rep"), None), P(("shard", "rep"), None), P("shard", None, None))
    return jax.shard_map(local, mesh=mesh, in_specs=in_specs, out_specs=out_specs, check_vma=False)
```

profile of v0, /device:TPU:1, one launch (start us, length us, event | category | flops | bytes accessed | tf_op | source)
XLA Modules:
  0.0 623.0 jit_solution(16797978285030678725)
XLA Ops:
  7.2 1.6 copy.14
  8.9 0.7 fusion.46
  9.7 0.7 bitcast_subtract_fusion.1
  16.2 0.7 add_bitcast_fusion
  17.0 4.0 broadcast_select_fusion
  21.0 109.1 %all-gather.2.cloned.1.call-done = bf16[2048,2,1152]{2,0,1:T(8,128)(2,1)} async-done(((bf16[32,2,1152]{2,0,1:T(8,128)(2,1)}), bf16[2048,2,1152]{2,0,1:T(8,128)(2,1)}) %all-gather.2.cloned.1.call-update) | async-done | bytes 9437200 | tf_op jit(solution)/shard_map/all_gather | solution.py:78
  130.1 8.2 %slice_bitcast_fusion = (bf16[2048,1152]{1,0:T(8,128)(2,1)}, bf16[2048,1152]{1,0:T(8,128)(2,1)}) fusion(bf16[2048,2,1152]{2,0,1:T(8,128)(2,1)} %all-gather.2.cloned.1.call-done), kind=kLoop, calls=%fused_computation.57 | loop fusion | bytes 18874368 | tf_op jit(solution)/shard_map/squeeze | solution.py:81
  138.3 1.6 broadcast.130.clone
  139.8 1.6 broadcast.130
  141.4 4.8 broadcast.131.clone
  146.2 24.7 %while.28 = (s32[]{:T(128)}, bf16[512,2048]{1,0:T(8,128)(2,1)}, bf16[512,2048]{1,0:T(8,128)(2,1)}, f32[2048,1152]{0,1:T(8,128)}, s32[]{:T(128)}, /*index=5*/s32[...) while((s32[]{:T(128)}, bf16[512,2048]{1,0:T(8,128)(2,1)}, ...), condition=%wide.region_3.4_spmd, body=%wide.region_2.3_spmd.sunk | while | flops 1818705920 | bytes 72974568 | solution.py:61
  146.9 2.6 fusion.87
  149.5 0.6 copy-done.1
  150.2 1.5 multiply_convert_fusion.8
  152.3 1.1 fusion.88
  153.5 3.8 dynamic_update_slice.17
  157.3 3.8 dynamic_update_slice.16
  161.1 1.7 fusion.89
  162.7 1.0 fusion.90
  163.8 7.1 %maximum_add_fusion.4 = f32[2048,1152]{0,1:T(8,128)} fusion(f32[2048,1152]{0,1:T(8,128)} %get-tuple-element.311, f32[2048,384]{0,1:T(8,128)S(1)} %fusion.89, f32[2048,768]{0,1:T(8,128)S(1)} %fusion.90), kind=kLoop, calls=%fused_computation.clone.1 | loop fusion | flops 4718592 | bytes 28311552 | tf_op jit(solution)/shard_map/while/body/add | solution.py:58
  170.9 9.6 %copy.15 = f32[2048,1152]{1,0:T(8,128)} copy(f32[2048,1152]{0,1:T(8,128)} %get-tuple-element.107) | data formatting | bytes 18874368 | tf_op jit(solution)/shard_map/while | solution.py:61
  180.5 4.8 broadcast.131
  185.4 49.4 %while.29 = (s32[]{:T(128)}, bf16[512,2048]{1,0:T(8,128)(2,1)}, bf16[512,2048]{1,0:T(8,128)(2,1)}, f32[2048,1152]{0,1:T(8,128)}, s32[]{:T(128)}, /*index=5*/s32[...) while((s32[]{:T(128)}, bf16[512,2048]{1,0:T(8,128)(2,1)}, ...), condition=%wide.region_5.6_spmd, body=%wide.region_4.5_spmd.sunk | while | flops 1818705920 | bytes 72974568 | solution.py:61
  186.0 2.6 fusion.99
  188.7 0.6 copy-done
  189.3 1.5 multiply_convert_fusion.9
  191.4 1.1 fusion.100
  192.6 3.8 dynamic_update_slice.19
  196.4 3.8 dynamic_update_slice.18
  200.2 1.7 fusion.101
  201.9 1.0 fusion.102
  202.9 7.1 %maximum_add_fusion.5 = f32[2048,1152]{0,1:T(8,128)} fusion(f32[2048,1152]{0,1:T(8,128)} %get-tuple-element.350, f32[2048,384]{0,1:T(8,128)S(1)} %fusion.101, f32[2048,768]{0,1:T(8,128)S(1)} %fusion.102), kind=kLoop, calls=%fused_computation.28.clone.1 | loop fusion | flops 4718592 | bytes 28311552 | tf_op jit(solution)/shard_map/while/body/add | solution.py:58
  210.7 2.6 fusion.99
  213.3 0.6 copy-done
  214.0 1.5 multiply_convert_fusion.9
  215.5 0.6 convolution_convert_fusion.5
  216.1 1.1 fusion.100
  217.3 3.8 dynamic_update_slice.19
  221.1 3.8 dynamic_update_slice.18
  224.9 1.7 fusion.101
  226.6 1.0 fusion.102
  227.6 7.1 %maximum_add_fusion.5 = f32[2048,1152]{0,1:T(8,128)} fusion(f32[2048,1152]{0,1:T(8,128)} %get-tuple-element.350, f32[2048,384]{0,1:T(8,128)S(1)} %fusion.101, f32[2048,768]{0,1:T(8,128)S(1)} %fusion.102), kind=kLoop, calls=%fused_computation.28.clone.1 | loop fusion | flops 4718592 | bytes 28311552 | tf_op jit(solution)/shard_map/while/body/add | solution.py:58
  234.7 9.7 %copy.16 = f32[2048,1152]{1,0:T(8,128)} copy(f32[2048,1152]{0,1:T(8,128)} %get-tuple-element.108) | data formatting | bytes 18874368 | tf_op jit(solution)/shard_map/while | solution.py:61
  244.5 14.5 %pad_maximum_fusion.6 = f32[2048,2,1152]{2,0,1:T(8,128)} fusion(f32[2048,1,1152]{2,0,1:T(8,128)} %bitcast.52, f32[2048,1,1152]{2,0,1:T(8,128)} %bitcast.51), kind=kLoop, calls=%fused_computation.56 | loop fusion | flops 4718592 | bytes 37748736 | tf_op jit(solution)/shard_map/stack | solution.py:90
  259.0 313.2 %reduce-scatter.2.cloned.1.call-done = f32[32,2,1152]{2,0,1:T(8,128)} async-done(((f32[2048,2,1152]{2,0,1:T(8,128)}), f32[32,2,1152]{2,0,1:T(8,128)}) %reduce-scatter.2.cloned.1.call-update) | async-done | bytes 294928 | tf_op jit(solution)/shard_map/reduce_scatter | solution.py:65
  572.2 1.6 convert_element_type.26
  573.9 40.8 %all-reduce.2.cloned.1.call-done = bf16[32,2,1152]{2,0,1:T(8,128)(2,1)} async-done(((bf16[32,2,1152]{2,0,1:T(8,128)(2,1)}), bf16[32,2,1152]{2,0,1:T(8,128)(2,1)}) %all-reduce.2.cloned.1.call-update) | async-done | bytes 147472 | tf_op jit(solution)/shard_map/psum | solution.py:66
  614.7 1.7 copy.17
  (14 shorter events, 2.3 us)
Async XLA Ops:
  7.2 122.9 %all-gather.2.cloned.1.call-start = ((), (), s32[]{:S(2)}) async-start(), calls=%async_computation.1 | async-start | bytes 9584640 | tf_op jit(solution)/shard_map/all_gather | solution.py:78
  8.8 563.4 %reduce-scatter.2.cloned.1.call-start = ((), (), s32[]{:S(2)}) async-start(), calls=%async_computation.2 | async-start | bytes 19169280 | tf_op jit(solution)/shard_map/reduce_scatter | solution.py:65
  146.9 3.3 copy-start.1
  186.0 3.3 copy-start
  210.7 3.3 copy-start
  259.0 355.8 %all-reduce.2.cloned.1.call-start = ((), (), s32[]{:S(2)}) async-start(), calls=%async_computation.3 | async-start | bytes 294912 | tf_op jit(solution)/shard_map/psum | solution.py:66
Sparse Core Ops, SparseCore 0:
  11.8 118.2 all-gather.1
  259.1 313.0 reduce-scatter.1
  575.6 39.0 all-reduce.1
where the time goes:
time: 624 us; the launch traced here: 623 us
  waiting for transfers between devices  463 us (74%)
  local copies, waits for them, and re-layouts  69 us (11%)
  other arithmetic  43.8 us (7%)
  matrix products  25.8 us (4%)
  between operations  19 us (3%)
    reduce_scatter x1, waiting for transfers between devices, reduce_grads(): lax.psum_scatter(grads, 'shard', scatter_dimension=0, tiled=True)  313 us
    all_gather x1, waiting for transfers between devices, local(): gathered = lax.all_gather(weights, 'shard', axis=0, tiled=True)  109 us
    psum x1, waiting for transfers between devices, reduce_grads(): return lax.psum(partial_sum.astype(jnp.bfloat16), 'rep').astype(jnp.float32)  40.8 us
    add x3, other arithmetic, block_step(): return (outputs, input_grads, grad_total + grad_piece)  21.4 us
    while x2, local copies, waits for them, and re-layouts, run_expert(): lax.fori_loop(jnp.int32(0), nblocks, block_step, (outputs, input_grads, s...  19.3 us
    another operation x1, other arithmetic, local(): reduced = reduce_grads(jnp.stack(pieces, axis=1))  14.5 us
    another operation x4, local copies, waits for them, and re-layouts  12.8 us
  transfers between devices with their start and end apart: 3, of which 3 were waited for; matrix products, arithmetic and copies ran while one was open for 1% of the time, Pallas kernels for 0%

commit v1 on v0

--- a/solution.py
+++ b/solution.py
@@ -63,7 +63,9 @@
 
 def reduce_grads(grads):
     partial_sum = lax.psum_scatter(grads, "shard", scatter_dimension=0, tiled=True)
-    return lax.psum(partial_sum.astype(jnp.bfloat16), "rep").astype(jnp.float32)
+    return jnp.sum(lax.all_gather(partial_sum.astype(jnp.bfloat16), "rep"), axis=0).astype(
+        jnp.float32
+    )
 
 
 def local(rows_in, cotangent, expert_counts, weights):

time: 624 us -> 597 us (0.957)
  waiting for transfers between devices: 463 us -> 424 us
  blocking collectives: 0 us -> 8.07 us
    psum x1 -> x0, waiting for transfers between devices: 40.8 us -> none  [reduce_grads(): return lax.psum(partial_sum.astype(jnp.bfloat16), 'rep').astype(jnp.float32)]
    all_gather x0 -> x1, blocking collectives: none -> 8.07 us  [reduce_grads(): lax.all_gather(partial_sum.astype(jnp.bfloat16), 'rep')]
  transfers between devices with their start and end apart: 3 -> 2, of which waited for: 3 -> 2; matrix products, arithmetic and copies ran while one was open for 1% -> 1% of each run, Pallas kernels for 0% -> 0%
where the time goes in v1:
time: 597 us; the launch traced here: 596 us
  waiting for transfers between devices  424 us (71%)
  local copies, waits for them, and re-layouts  68 us (11%)
  other arithmetic  42.8 us (7%)
  matrix products  31.5 us (5%)
  between operations  19.3 us (3%)
  blocking collectives  8.07 us (1%)
    reduce_scatter x1, waiting for transfers between devices, reduce_grads(): lax.psum_scatter(grads, 'shard', scatter_dimension=0, tiled=True)  315 us
    all_gather x1, waiting for transfers between devices, local(): gathered = lax.all_gather(weights, 'shard', axis=0, tiled=True)  109 us
    add x3, other arithmetic, block_step(): return (outputs, input_grads, grad_total + grad_piece)  21 us
    while x2, local copies, waits for them, and re-layouts, run_expert(): lax.fori_loop(jnp.int32(0), nblocks, block_step, (outputs, input_grads, s...  19.3 us
    another operation x1, other arithmetic, local(): reduced = reduce_grads(jnp.stack(pieces, axis=1))  14.4 us
    another operation x4, local copies, waits for them, and re-layouts  12.8 us
  transfers between devices with their start and end apart: 2, of which 2 were waited for; matrix products, arithmetic and copies ran while one was open for 1% of the time, Pallas kernels for 0%

profile of v1, /device:TPU:1, one launch (start us, length us, event | category | flops | bytes accessed | tf_op | source)
XLA Modules:
  0.0 595.9 jit_solution(16863539288652338063)
XLA Ops:
  7.2 1.6 copy.15
  8.9 0.7 fusion.46
  9.7 0.7 bitcast_subtract_fusion.1
  16.2 0.7 add_bitcast_fusion
  17.0 4.0 broadcast_select_fusion
  20.9 109.2 %all-gather.3.cloned.1.call-done = bf16[2048,2,1152]{2,0,1:T(8,128)(2,1)} async-done(((bf16[32,2,1152]{2,0,1:T(8,128)(2,1)}), bf16[2048,2,1152]{2,0,1:T(8,128)(2,1)}) %all-gather.3.cloned.1.call-update) | async-done | bytes 9437200 | tf_op jit(solution)/shard_map/all_gather | solution.py:80
  130.1 8.1 %slice_bitcast_fusion = (bf16[2048,1152]{1,0:T(8,128)(2,1)}, bf16[2048,1152]{1,0:T(8,128)(2,1)}) fusion(bf16[2048,2,1152]{2,0,1:T(8,128)(2,1)} %all-gather.3.cloned.1.call-done), kind=kLoop, calls=%fused_computation.57 | loop fusion | bytes 18874368 | tf_op jit(solution)/shard_map/squeeze | solution.py:83
  138.2 1.6 broadcast.130
  139.8 1.6 broadcast.130.clone
  141.4 4.8 broadcast.131.clone
  146.2 26.4 %while.28 = (s32[]{:T(128)}, bf16[512,2048]{1,0:T(8,128)(2,1)}, bf16[512,2048]{1,0:T(8,128)(2,1)}, f32[2048,1152]{0,1:T(8,128)}, s32[]{:T(128)}, /*index=5*/s32[...) while((s32[]{:T(128)}, bf16[512,2048]{1,0:T(8,128)(2,1)}, ...), condition=%wide.region_3.4_spmd, body=%wide.region_2.3_spmd.sunk | while | flops 1818705920 | bytes 72974576 | solution.py:61
  146.8 2.6 fusion.87
  149.5 0.6 copy-done.1
  150.1 1.5 multiply_convert_fusion.8
  151.6 0.6 convolution_convert_fusion.4
  152.3 3.8 dynamic_update_slice.16
  156.1 3.0 fusion.88
  159.1 3.8 dynamic_update_slice.17
  162.9 1.7 fusion.89
  164.6 1.0 fusion.90
  165.6 7.0 %maximum_add_fusion.4 = f32[2048,1152]{0,1:T(8,128)} fusion(f32[2048,1152]{0,1:T(8,128)} %get-tuple-element.311, f32[2048,384]{0,1:T(8,128)S(1)} %fusion.89, f32[2048,768]{0,1:T(8,128)S(1)} %fusion.90), kind=kLoop, calls=%fused_computation.clone.1 | loop fusion | flops 4718592 | bytes 28311552 | tf_op jit(solution)/shard_map/while/body/add | solution.py:58
  172.6 4.8 broadcast.131
  177.5 52.9 %while.29 = (s32[]{:T(128)}, bf16[512,2048]{1,0:T(8,128)(2,1)}, bf16[512,2048]{1,0:T(8,128)(2,1)}, f32[2048,1152]{0,1:T(8,128)}, s32[]{:T(128)}, /*index=5*/s32[...) while((s32[]{:T(128)}, bf16[512,2048]{1,0:T(8,128)(2,1)}, ...), condition=%wide.region_5.6_spmd, body=%wide.region_4.5_spmd.sunk | while | flops 1818705920 | bytes 72974576 | solution.py:61
  178.1 2.6 fusion.99
  180.7 0.6 copy-done
  181.4 1.5 multiply_convert_fusion.9
  183.5 3.8 dynamic_update_slice.18
  187.3 3.0 fusion.100
  190.4 3.8 dynamic_update_slice.19
  194.2 1.7 fusion.101
  195.9 1.0 fusion.102
  196.9 7.0 %maximum_add_fusion.5 = f32[2048,1152]{0,1:T(8,128)} fusion(f32[2048,1152]{0,1:T(8,128)} %get-tuple-element.350, f32[2048,384]{0,1:T(8,128)S(1)} %fusion.101, f32[2048,768]{0,1:T(8,128)S(1)} %fusion.102), kind=kLoop, calls=%fused_computation.28.clone.1 | loop fusion | flops 4718592 | bytes 28311552 | tf_op jit(solution)/shard_map/while/body/add | solution.py:58
  204.6 2.6 fusion.99
  207.2 0.6 copy-done
  207.8 1.5 multiply_convert_fusion.9
  210.0 3.8 dynamic_update_slice.18
  213.8 3.0 fusion.100
  216.8 3.8 dynamic_update_slice.19
  220.6 1.7 fusion.101
  222.3 1.0 fusion.102
  223.3 7.0 %maximum_add_fusion.5 = f32[2048,1152]{0,1:T(8,128)} fusion(f32[2048,1152]{0,1:T(8,128)} %get-tuple-element.350, f32[2048,384]{0,1:T(8,128)S(1)} %fusion.101, f32[2048,768]{0,1:T(8,128)S(1)} %fusion.102), kind=kLoop, calls=%fused_computation.28.clone.1 | loop fusion | flops 4718592 | bytes 28311552 | tf_op jit(solution)/shard_map/while/body/add | solution.py:58
  230.3 9.7 %copy.17 = f32[2048,1152]{1,0:T(8,128)} copy(f32[2048,1152]{0,1:T(8,128)} %get-tuple-element.108) | data formatting | bytes 18874368 | tf_op jit(solution)/shard_map/while | solution.py:61
  240.0 9.6 %copy.16 = f32[2048,1152]{1,0:T(8,128)} copy(f32[2048,1152]{0,1:T(8,128)} %get-tuple-element.107) | data formatting | bytes 18874368 | tf_op jit(solution)/shard_map/while | solution.py:61
  249.6 14.4 %pad_maximum_fusion.6 = f32[2048,2,1152]{2,0,1:T(8,128)} fusion(f32[2048,1,1152]{2,0,1:T(8,128)} %bitcast.52, f32[2048,1,1152]{2,0,1:T(8,128)} %bitcast.53), kind=kLoop, calls=%fused_computation.56 | loop fusion | flops 4718592 | bytes 37748736 | tf_op jit(solution)/shard_map/stack | solution.py:92
  264.1 314.9 %reduce-scatter.2.cloned.1.call-done = f32[32,2,1152]{2,0,1:T(8,128)} async-done(((f32[2048,2,1152]{2,0,1:T(8,128)}), f32[32,2,1152]{2,0,1:T(8,128)}) %reduce-scatter.2.cloned.1.call-update) | async-done | bytes 294928 | tf_op jit(solution)/shard_map/reduce_scatter | solution.py:65
  579.1 1.0 convert_element_type.28
  580.0 8.1 %all-gather = bf16[128,2,1152]{2,0,1:T(8,128)(2,1)S(1)} all-gather(bf16[32,2,1152]{2,0,1:T(8,128)(2,1)S(1)} %convert_element_type.28), channel_id=2, replica_groups=mesh['shard'=64,'rep'=4] {'rep'}, dimensions={0}, use_global_device_ids=true | all-gather | bytes 737280 | tf_op jit(solution)/shard_map/all_gather | solution.py:66
  588.2 0.8 copy.18
  (13 shorter events, 2.3 us)
Async XLA Ops:
  7.2 122.9 %all-gather.3.cloned.1.call-start = ((), (), s32[]{:S(2)}) async-start(), calls=%async_computation.1 | async-start | bytes 9584640 | tf_op jit(solution)/shard_map/all_gather | solution.py:80
  8.8 570.2 %reduce-scatter.2.cloned.1.call-start = ((), (), s32[]{:S(2)}) async-start(), calls=%async_computation.2 | async-start | bytes 19169280 | tf_op jit(solution)/shard_map/reduce_scatter | solution.py:65
  146.8 3.3 copy-start.1
  178.1 3.3 copy-start
  204.5 3.3 copy-start
Sparse Core Ops, SparseCore 0:
  11.8 118.2 all-gather.2
  264.2 314.7 reduce-scatter.1
